TPU v7x, 128 devices: a whole 4x4x4 slice. The times are simulated.
128 devices in a mesh: frow: 16 (over y, z), fcol: 8 (over x, core).
Axes of the slice: x: 4, y: 4, z: 4, core: 2. Of those that a mesh axis runs over, the one named last changes fastest.
Arguments:
- front_orig: float32 [16, 1024, 8, 2048], P('frow', None, 'fcol'), may hold values from -0.1 to 45, as said below
- child_tiles: bfloat16 [8192, 128, 128], P(('frow', 'fcol')), may hold values from -0.25 to 0.25
- tile_target: int32 [8192, 2], P(('frow', 'fcol')), may hold values from 0 to 127, as said below
- tile_rows: int32 [8192, 128], P(('frow', 'fcol')), may hold values from 0 to 127, each once within a row
- tile_cols: int32 [8192, 128], P(('frow', 'fcol')), may hold values from 0 to 127, each once within a row
Outputs:
- front_out: float32 [16, 1024, 8, 2048], P('frow', None, 'fcol')
Inputs may be any that keep to these rules, and one draw needn't show every extreme that they name: `front_orig`: Symmetric; the lower triangle of the front after every tile is added defines a positive definite matrix. `tile_target`: rows come 64 to a device in device order. Column 0 is the owner, frow index times 8 plus fcol index; column 1 the local block on that owner, local block row times 16 plus local block column; the block lies on or below the front's block diagonal. At most 2 tiles of one device go to one owner, and one owner receives exactly 2 from every device.
All inputs are finite; a program needn't handle non-finite values.
Results may differ from a plain program's by a relative error of at most 0.0003.
Values may be sent and summed in bfloat16 or wider, within the bound.
No kernel may reach another device: no remote copies, remote signals or barrier semaphores. Data moves between devices by JAX's collectives and lax.ppermute only.
A program may use at most 128 MiB of HBM per device.

v0:
```python
import jax
import jax.numpy as jnp
from jax import lax
from jax.sharding import PartitionSpec as P

PW = 512
NPANEL = 2
CAP = 2


def as_sent(x):
    return jax.tree.map(lambda a: a.astype(jnp.bfloat16) if a.dtype == jnp.float32 else a, x)


def broadcast(block, axis, source):
    block = jnp.where(lax.axis_index(axis) == source, block, jnp.zeros_like(block))
    return lax.psum(block, axis)


def place_tiles(received):
    tile_block, perm_block, target_block = received
    width = tile_block.shape[-1]
    positions = jnp.arange(width, dtype=jnp.int32)
    row_onehot = (perm_block[:, :, 0, None, :] == positions[:, None]).astype(jnp.bfloat16)
    col_onehot = (perm_block[:, :, 1, None, :] == positions[:, None]).astype(jnp.bfloat16)
    moved = jnp.einsum(
        "abxi,abij->abxj", row_onehot, tile_block, preferred_element_type=jnp.float32
    ).astype(jnp.bfloat16)
    placed = jnp.einsum(
        "abxj,abyj->abxy", moved, col_onehot, preferred_element_type=jnp.float32
    ).astype(jnp.bfloat16)
    return (placed, target_block)


def subtract_product(matrix, row_factor, col_factor):
    product = jnp.dot(
        row_factor, col_factor.T, precision=lax.Precision.HIGH, preferred_element_type=jnp.float32
    )
    return matrix - product


def shards(front_orig, child_tiles, tile_target, tile_rows, tile_cols):
    row_devs = lax.axis_size("frow")
    col_devs = lax.axis_size("fcol")
    owners = row_devs * col_devs
    row_here = lax.axis_index("frow")
    col_here = lax.axis_index("fcol")
    width = child_tiles.shape[1]
    held = child_tiles.shape[0]
    slot_count = owners * CAP
    owner_of = tile_target[:, 0]
    block_of = tile_target[:, 1]
    tile_order = jnp.arange(held, dtype=jnp.int32)
    same_owner = owner_of[:, None] == owner_of[None, :]
    earlier = tile_order[None, :] < tile_order[:, None]
    rank_of = jnp.sum(jnp.where(same_owner & earlier, 1, 0), axis=1).astype(jnp.int32)
    slot_of = owner_of * CAP + rank_of
    slot_match = slot_of[None, :] == jnp.arange(slot_count, dtype=jnp.int32)[:, None]
    source_tile = jnp.sum(jnp.where(slot_match, tile_order[None, :], 0), axis=1)
    filled = jnp.any(slot_match, axis=1)
    own_perms = jnp.stack([tile_rows, tile_cols], axis=1)
    placed_here, _ = place_tiles((child_tiles[None], own_perms[None], block_of[None]))
    placed_here = placed_here[0]
    send_tiles = jnp.where(
        filled[:, None, None],
        jnp.take(placed_here, source_tile, axis=0),
        jnp.zeros((), jnp.bfloat16),
    )
    send_blocks = jnp.where(filled, jnp.take(block_of, source_tile, axis=0), -1)
    placed = lax.all_to_all(
        send_tiles.reshape(owners, CAP, width, width),
        ("frow", "fcol"),
        split_axis=0,
        concat_axis=0,
        tiled=True,
    )
    blocks_in = lax.all_to_all(
        send_blocks.reshape(owners, CAP), ("frow", "fcol"), split_axis=0, concat_axis=0, tiled=True
    )
    local = front_orig[0, :, 0, :]
    row_blocks = local.shape[0] // width
    col_blocks = local.shape[1] // width
    block_ids = jnp.arange(row_blocks * col_blocks, dtype=jnp.int32)
    block_onehot = (blocks_in.reshape(1, slot_count) == block_ids[:, None]).astype(jnp.bfloat16)
    summed = jnp.dot(
        block_onehot, placed.reshape(slot_count, width * width), preferred_element_type=jnp.float32
    )
    added = (
        summed.reshape(row_blocks, col_blocks, width, width)
        .transpose(0, 2, 1, 3)
        .reshape(local.shape)
    )
    matrix = local + added
    first_ids = jnp.arange(row_blocks, dtype=jnp.int32) * col_blocks
    first_onehot = (blocks_in.reshape(1, slot_count) == first_ids[:, None]).astype(jnp.bfloat16)
    first_added = jnp.dot(
        first_onehot, placed.reshape(slot_count, width * width), preferred_element_type=jnp.float32
    ).reshape(local.shape[0], width)
    first_column = local[:, :width] + first_added
    local_rows = jnp.arange(local.shape[0], dtype=jnp.int32)
    local_cols = jnp.arange(local.shape[1], dtype=jnp.int32)
    global_rows = (local_rows // width * row_devs + row_here) * width + local_rows % width
    global_cols = (local_cols // width * col_devs + col_here) * width + local_cols % width
    total = NPANEL * PW
    hi = lax.Precision.HIGH
    first_row = lax.all_gather(
        first_column[:width].astype(jnp.bfloat16), "fcol", axis=1, tiled=True
    )[:, :total]
    split = total // 2
    left = lax.all_gather(first_row[:, :split], "frow", axis=0, tiled=True)[:total]
    left, right_src, matrix = lax.optimization_barrier((left, first_row[:, split:], matrix))
    right = lax.all_gather(right_src, "frow", axis=0, tiled=True)[:total]
    right, own_column = lax.optimization_barrier((right, first_column))
    halves = [left.astype(jnp.float32), right.astype(jnp.float32)]
    row_panel = lax.all_gather(own_column.astype(jnp.bfloat16), "fcol", axis=1, tiled=True)[
        :, :total
    ]
    half = row_devs // col_devs
    pairs = []
    for src_row in range(row_devs):
        for src_col in range(col_devs):
            dst_row = src_row // col_devs * col_devs + src_col
            dst_col = src_row % col_devs
            pairs.append((src_row * col_devs + src_col, dst_row * col_devs + dst_col))
    piece = lax.dynamic_slice_in_dim(row_panel, col_here * width, width, axis=0)
    piece = lax.ppermute(piece, ("frow", "fcol"), pairs)
    col_all = lax.all_gather(piece, "frow", axis=0, tiled=False)
    col_panel = (
        col_all.reshape(half, row_blocks, width, total)
        .transpose(1, 0, 2, 3)
        .reshape(local.shape[1], total)
    )
    rows_all = jnp.concatenate([row_panel, col_panel], axis=0).astype(jnp.float32)
    n_own = local.shape[0]
    full = lax.Precision.HIGHEST
    corner_blocks = total // width
    factor_full = jnp.zeros((total, total), jnp.float32)
    eye = jnp.eye(width, dtype=jnp.float32)
    inverses = []
    for h, cur in enumerate(halves):
        if h > 0:
            done_cols = factor_full[:, : h * split]
            cur = cur - jnp.dot(
                done_cols,
                done_cols[h * split : (h + 1) * split].T,
                precision=full,
                preferred_element_type=jnp.float32,
            )
        for b in range(split // width):
            start = h * split + b * width
            stop = start + width
            lb = b * width
            diag_block = cur[start:stop, lb : lb + width]
            symmetric = jnp.tril(diag_block) + jnp.tril(diag_block, -1).T
            factor = jnp.linalg.cholesky(symmetric)
            inverse = lax.linalg.triangular_solve(factor, eye, left_side=True, lower=True)
            inverses.append(inverse)
            factor_full = factor_full.at[start:stop, start:stop].set(factor)
            if stop < total:
                below = jnp.dot(
                    cur[stop:, lb : lb + width],
                    inverse.T,
                    precision=full,
                    preferred_element_type=jnp.float32,
                )
                factor_full = factor_full.at[stop:, start:stop].set(below)
                if lb + width < split:
                    cur = cur.at[stop:, lb + width :].add(
                        -jnp.dot(
                            below,
                            below[: split - lb - width].T,
                            precision=full,
                            preferred_element_type=jnp.float32,
                        )
                    )
    inv_blocks = jnp.stack(inverses)
    size = width
    while size < total:
        pairs_n = total // (2 * size)
        lower_left = jnp.stack(
            [
                factor_full[
                    (2 * k + 1) * size : (2 * k + 2) * size, 2 * k * size : (2 * k + 1) * size
                ]
                for k in range(pairs_n)
            ]
        )
        upper_inv = inv_blocks[0::2]
        lower_inv = inv_blocks[1::2]
        mixed = -jnp.einsum(
            "nab,nbc->nac",
            lower_inv,
            jnp.einsum("nab,nbc->nac", lower_left, upper_inv, precision=full),
            precision=full,
        )
        zeros = jnp.zeros_like(mixed)
        top = jnp.concatenate([upper_inv, zeros], axis=2)
        bottom = jnp.concatenate([mixed, lower_inv], axis=2)
        inv_blocks = jnp.concatenate([top, bottom], axis=1)
        size *= 2
    factor_inverse = inv_blocks[0]
    solved = jnp.dot(rows_all, factor_inverse.T, precision=hi, preferred_element_type=jnp.float32)
    row_factor = solved[:n_own]
    col_factor = solved[n_own:]
    matrix = subtract_product(matrix, row_factor, col_factor)
    corner_rows = lax.dynamic_slice_in_dim(
        factor_full, jnp.minimum(row_here, total // width - 1) * width, width, axis=0
    )
    head = jnp.where(row_here * width < total, corner_rows, row_factor[:width])
    panel_vals = jnp.concatenate([head, row_factor[width:]], axis=0)
    own_part = lax.dynamic_slice_in_dim(panel_vals, col_here * width, width, axis=1)
    matrix = matrix.at[:, :width].set(own_part)
    lower_part = global_rows[:, None] >= global_cols[None, :]
    result = jnp.where(lower_part, matrix, 0.0)
    return result[None, :, None, :]


def solution(mesh):
    return jax.shard_map(
        shards,
        mesh=mesh,
        in_specs=(
            P("frow", None, "fcol", None),
            P(("frow", "fcol"), None, None),
            P(("frow", "fcol"), None),
            P(("frow", "fcol"), None),
            P(("frow", "fcol"), None),
        ),
        out_specs=P("frow", None, "fcol", None),
        check_vma=False,
    )
```

profile of v0, /device:TPU:23, one launch (start us, length us, event | category | flops | bytes accessed | tf_op | source)
XLA Modules:
  0.0 611.7 jit_solution(1710537951863947196)
XLA Ops:
  11.4 10.6 %all-to-all-start = ((s32[128,1,2]{2,1,0:T(1,128)}), s32[128,1,2]{2,1,0:T(1,128)S(1)}, u32[]{:S(2)}, u32[]{:S(2)}) async-start(s32[128,1,2]{2,1,0:T(1,128)} %bitcast.5), calls=%async_computation | async-start | bytes 131072 | tf_op jit(solution)/shard_map/all_to_all | solution.py:77
  26.8 10.2 %gather_fusion.1 = bf16[256,128,128]{2,1,0:T(8,128)(2,1)} fusion(bf16[64,128,128]{2,1,0:T(8,128)(2,1)} %fusion.28, s32[1024]{0:T(1024)S(1)} %pad_clamp_fusion), kind=kCustom, calls=%fused_computation.1 | custom fusion | bytes 16778240 | tf_op jit(solution)/shard_map/jit(_take)/gather | solution.py:66
  44.4 10.2 %all-to-all-start.1 = ((bf16[128,2,128,128]{3,2,1,0:T(8,128)(2,1)}), bf16[128,2,128,128]{3,2,1,0:T(8,128)(2,1)}, u32[]{:S(2)}, u32[]{:S(2)}) async-start(bf16[128,2,128,128]{3,2,1,0:T(8,128)(2,1)} %select_select_fusion), calls=%async_computation.1 | async-start | bytes 16777216 | tf_op jit(solution)/shard_map/all_to_all | solution.py:70
  55.0 20.7 %copy.246 = f32[1,1024,1,2048]{1,3,2,0:T(8,128)} copy(f32[1,1024,1,2048]{3,2,1,0:T(1,128)} %param.52) | data formatting | bytes 16777216 | tf_op args[0]
  77.0 76.1 %all-to-all-done.1 = bf16[128,2,128,128]{3,2,1,0:T(8,128)(2,1)} async-done(((bf16[128,2,128,128]{3,2,1,0:T(8,128)(2,1)}), bf16[128,2,128,128]{3,2,1,0:T(8,128)(2,1)}, u32[]{:S(2)}, u32[]{:S(2)}) %all-to-all-start.1) | async-done | bytes 8388640 | tf_op jit(solution)/shard_map/all_to_all | solution.py:70
  153.1 7.8 %fusion.143 = f32[8,16384]{1,0:T(8,128)S(1)} fusion(s32[256]{0:T(256)S(1)} %eq.128, s32[8]{0:T(128)S(1)} %iota_multiply_fusion, bf16[32,8,128,128]{3,2,1,0:T(8,128)(2,1)} %bitcast.76), kind=kOutput, calls=%fused_computation.238 | convolution fusion | flops 67110912 | bytes 8913952 | tf_op jit(solution)/shard_map/dot_general | solution.py:96
  162.4 18.7 %all_gather.18 = bf16[128,1024]{0,1:T(8,128)(2,1)S(1)} all-gather(bf16[128,128]{0,1:T(8,128)(2,1)S(1)} %slice.839), channel_id=1, replica_groups=mesh['frow'=16,'fcol'=8] {'fcol'}, dimensions={1}, use_global_device_ids=true | all-gather | bytes 294912 | tf_op jit(solution)/shard_map/all_gather | solution.py:106
  184.6 23.3 %copy.365 = bf16[32,8,128,128]{3,1,2,0:T(8,128)(2,1)} copy(bf16[32,8,128,128]{3,2,1,0:T(8,128)(2,1)} %bitcast.76) | data formatting | bytes 16777216
  207.9 11.9 %copy.249 = bf16[256,16384]{0,1:T(8,128)(2,1)} copy(bf16[256,16384]{1,0:T(8,128)(2,1)} %bitcast.218) | data formatting | bytes 16777216 | tf_op jit(solution)/shard_map/reshape | solution.py:97
  226.1 7.5 %copy.364 = f32[128,8,16,128]{3,1,2,0:T(8,128)} copy(f32[128,8,16,128]{3,2,1,0:T(8,128)S(1)} %bitcast.222) | data formatting | bytes 16777216
  233.6 9.3 %copy.343 = f32[1024,2048]{0,1:T(8,128)} copy(f32[1024,2048]{1,0:T(8,128)} %bitcast.219) | data formatting | bytes 16777216 | tf_op jit(solution)/shard_map/reshape | solution.py:91
  242.9 12.1 %bitcast_add_fusion.16 = f32[1024,2048]{0,1:T(8,128)} fusion(f32[1024,2048]{0,1:T(8,128)} %copy.343, f32[1,1024,1,2048]{1,3,2,0:T(8,128)} %copy.246), kind=kLoop, calls=%fused_computation.280 | loop fusion | flops 2097152 | bytes 25165824 | tf_op jit(solution)/shard_map/add | solution.py:93
  257.4 11.7 %cholesky.134 = f32[128,128]{1,0:T(8,128)S(1)} custom-call(f32[128,128]{1,0:T(8,128)S(1)} %copy.258), custom_call_target="Cholesky" | custom-call | tf_op jit(solution)/shard_map/jit(cholesky)/cholesky | solution.py:155
  270.9 9.8 %custom-call.12 = f32[1,128,128]{1,2,0:T(8,128)S(1)} custom-call(f32[1,128,128]{2,1,0:T(8,128)S(1)} %copy.261), custom_call_target="InvertDiagBlocksLowerTriangular" | custom-call | tf_op jit(solution)/shard_map/triangular_solve/custom-call.0 | solution.py:156
  288.2 11.9 %cholesky.145 = f32[128,128]{1,0:T(8,128)S(1)} custom-call(f32[128,128]{1,0:T(8,128)S(1)} %copy.268), custom_call_target="Cholesky" | custom-call | tf_op jit(solution)/shard_map/jit(cholesky)/cholesky | solution.py:155
  305.8 9.8 %custom-call.13 = f32[1,128,128]{1,2,0:T(8,128)S(1)} custom-call(f32[1,128,128]{2,1,0:T(8,128)S(1)} %copy.271), custom_call_target="InvertDiagBlocksLowerTriangular" | custom-call | tf_op jit(solution)/shard_map/triangular_solve/custom-call.0 | solution.py:156
  318.6 11.7 %cholesky.156 = f32[128,128]{1,0:T(8,128)S(1)} custom-call(f32[128,128]{1,0:T(8,128)S(1)} %copy.278), custom_call_target="Cholesky" | custom-call | tf_op jit(solution)/shard_map/jit(cholesky)/cholesky | solution.py:155
  333.5 9.8 %custom-call.14 = f32[1,128,128]{1,2,0:T(8,128)S(1)} custom-call(f32[1,128,128]{2,1,0:T(8,128)S(1)} %copy.281), custom_call_target="InvertDiagBlocksLowerTriangular" | custom-call | tf_op jit(solution)/shard_map/triangular_solve/custom-call.0 | solution.py:156
  346.2 11.7 %cholesky.167 = f32[128,128]{1,0:T(8,128)S(1)} custom-call(f32[128,128]{1,0:T(8,128)S(1)} %fusion.105), custom_call_target="Cholesky" | custom-call | tf_op jit(solution)/shard_map/jit(cholesky)/cholesky | solution.py:155
  361.0 9.8 %custom-call.15 = f32[1,128,128]{1,2,0:T(8,128)S(1)} custom-call(f32[1,128,128]{2,1,0:T(8,128)S(1)} %copy.288), custom_call_target="InvertDiagBlocksLowerTriangular" | custom-call | tf_op jit(solution)/shard_map/triangular_solve/custom-call.0 | solution.py:156
  381.7 11.7 %cholesky.178 = f32[128,128]{1,0:T(8,128)S(1)} custom-call(f32[128,128]{1,0:T(8,128)S(1)} %fusion.103), custom_call_target="Cholesky" | custom-call | tf_op jit(solution)/shard_map/jit(cholesky)/cholesky | solution.py:155
  395.6 9.8 %custom-call.16 = f32[1,128,128]{1,2,0:T(8,128)S(1)} custom-call(f32[1,128,128]{2,1,0:T(8,128)S(1)} %copy.299), custom_call_target="InvertDiagBlocksLowerTriangular" | custom-call | tf_op jit(solution)/shard_map/triangular_solve/custom-call.0 | solution.py:156
  412.1 16.0 %collective-permute-done = bf16[128,1024]{0,1:T(8,128)(2,1)S(1)} collective-permute-done((bf16[128,1024]{0,1:T(8,128)(2,1)S(1)}, bf16[128,1024]{0,1:T(8,128)(2,1)S(1)}, u32[]{:S(2)}, u32[]{:S(2)}) %collective-permute-start) | collective-permute-done | bytes 262176 | tf_op jit(solution)/shard_map/ppermute | solution.py:126
  429.0 11.7 %cholesky.189 = f32[128,128]{1,0:T(8,128)S(1)} custom-call(f32[128,128]{1,0:T(8,128)S(1)} %fusion.101), custom_call_target="Cholesky" | custom-call | tf_op jit(solution)/shard_map/jit(cholesky)/cholesky | solution.py:155
  443.7 9.8 %custom-call.17 = f32[1,128,128]{1,2,0:T(8,128)S(1)} custom-call(f32[1,128,128]{2,1,0:T(8,128)S(1)} %copy.305), custom_call_target="InvertDiagBlocksLowerTriangular" | custom-call | tf_op jit(solution)/shard_map/triangular_solve/custom-call.0 | solution.py:156
  454.9 11.7 %cholesky.200 = f32[128,128]{1,0:T(8,128)S(1)} custom-call(f32[128,128]{1,0:T(8,128)S(1)} %fusion.99), custom_call_target="Cholesky" | custom-call | tf_op jit(solution)/shard_map/jit(cholesky)/cholesky | solution.py:155
  469.5 10.0 %custom-call.18 = f32[1,128,128]{1,2,0:T(8,128)S(1)} custom-call(f32[1,128,128]{2,1,0:T(8,128)S(1)} %copy.311), custom_call_target="InvertDiagBlocksLowerTriangular" | custom-call | tf_op jit(solution)/shard_map/triangular_solve/custom-call.0 | solution.py:156
  480.8 11.7 %cholesky.211 = f32[128,128]{1,0:T(8,128)S(1)} custom-call(f32[128,128]{1,0:T(8,128)S(1)} %fusion.97), custom_call_target="Cholesky" | custom-call | tf_op jit(solution)/shard_map/jit(cholesky)/cholesky | solution.py:155
  493.8 9.8 %custom-call.19 = f32[1,128,128]{1,2,0:T(8,128)S(1)} custom-call(f32[1,128,128]{2,1,0:T(8,128)S(1)} %get-tuple-element.281), custom_call_target="InvertDiagBlocksLowerTriangular" | custom-call | tf_op jit(solution)/shard_map/triangular_solve/custom-call.0 | solution.py:156
  532.9 16.6 %fusion.2 = f32[3072,1024]{1,0:T(8,128)S(1)} fusion(bf16[2048,1024]{1,0:T(8,128)(2,1)} %bitcast.224, bf16[1024,1024]{1,0:T(8,128)(2,1)S(1)} %copy.252, f32[1,512,512]{2,1,0:T(8,128)} %get-tuple-element.292, f32[1,512,512]{2,1,0:T(8,128)} %get-tuple-element.291, f32[1,512,512]{2,1,0:T(8,128)S(1)} %fusion.35), kind=kOutput, calls=%fused_computation.8 | convolution fusion | flops 19344130048 | bytes 22020096 | tf_op jit(solution)/shard_map/dot_general | solution.py:202
  551.9 17.7 %fusion.15 = f32[1024,2048]{0,1:T(8,128)} fusion(f32[1024,2048]{0,1:T(8,128)} %bitcast_add_fusion.16, f32[3072,1024]{1,0:T(8,128)S(1)} %fusion.2), kind=kOutput, calls=%fused_computation.26 | convolution fusion | flops 12886999040 | bytes 29360128 | tf_op jit(solution)/shard_map/dot_general | solution.py:36
  584.5 20.5 %copy.329 = f32[1,1024,1,2048]{3,2,1,0:T(1,128)} copy(f32[1,1024,1,2048]{1,3,2,0:T(8,128)} %select_bitcast_fusion) | data formatting | bytes 16777216 | tf_op jit(solution)/shard_map/broadcast_in_dim | solution.py:215
  (224 shorter events, 135.6 us)
Async XLA Ops:
  6.5 16.6 %copy-start = (bf16[64,128,128]{2,1,0:T(8,128)(2,1)S(1)}, bf16[64,128,128]{2,1,0:T(8,128)(2,1)}, u32[]{:S(2)}) copy-start(bf16[64,128,128]{2,1,0:T(8,128)(2,1)} %param.53) | copy-start | bytes 6291460
  11.4 33.0 %all-to-all-start = ((s32[128,1,2]{2,1,0:T(1,128)}), s32[128,1,2]{2,1,0:T(1,128)S(1)}, u32[]{:S(2)}, u32[]{:S(2)}) async-start(s32[128,1,2]{2,1,0:T(1,128)} %bitcast.5), calls=%async_computation | async-start | bytes 131072 | tf_op jit(solution)/shard_map/all_to_all | solution.py:77
  44.4 108.7 %all-to-all-start.1 = ((bf16[128,2,128,128]{3,2,1,0:T(8,128)(2,1)}), bf16[128,2,128,128]{3,2,1,0:T(8,128)(2,1)}, u32[]{:S(2)}, u32[]{:S(2)}) async-start(bf16[128,2,128,128]{3,2,1,0:T(8,128)(2,1)} %select_select_fusion), calls=%async_computation.1 | async-start | bytes 16777216 | tf_op jit(solution)/shard_map/all_to_all | solution.py:70
  54.6 200.4 %all-gather.6.cloned.1.call-start = ((), (), s32[]{:S(2)}) async-start(), calls=%async_computation.2 | async-start | bytes 2228224 | tf_op jit(solution)/shard_map/all_gather | solution.py:110
  162.3 45.6 %copy-start.5 = (bf16[1024,128]{0,1:T(8,128)(2,1)}, bf16[1024,128]{0,1:T(8,128)(2,1)S(1)}, u32[]{:S(2)}) copy-start(bf16[1024,128]{0,1:T(8,128)(2,1)S(1)} %slice_add_fusion) | copy-start | bytes 786436
  181.8 162.5 %all-gather.8.cloned.1.call-start = ((), (), s32[]{:S(2)}) async-start(), calls=%async_computation.3 | async-start | bytes 2228224 | tf_op jit(solution)/shard_map/all_gather | solution.py:112
  181.9 26.0 %copy-start.10 = (s32[128]{0:T(128)}, s32[128]{0:T(128)S(1)}, u32[]{:S(2)}) copy-start(s32[128]{0:T(128)S(1)} %iota_add_fusion) | copy-start | bytes 1540
  182.1 75.1 %copy-start.6 = (pred[128,128]{0,1:T(8,128)(4,1)}, pred[128,128]{0,1:T(8,128)(4,1)S(1)}, u32[]{:S(2)}) copy-start(pred[128,128]{0,1:T(8,128)(4,1)S(1)} %copy.255) | copy-start | bytes 49156
  256.6 150.5 %all-gather.10.cloned.1.call-start = ((), (), s32[]{:S(2)}) async-start(), calls=%async_computation.4 | async-start | bytes 2359296 | tf_op jit(solution)/shard_map/all_gather | solution.py:115
  287.1 16.4 %copy-start.4 = (f32[896,128]{0,1:T(8,128)S(1)}, f32[896,128]{0,1:T(8,128)}, u32[]{:S(2)}) copy-start(f32[896,128]{0,1:T(8,128)} %copy.289) | copy-start | bytes 1376260
  300.2 18.2 %copy-start.7 = (pred[128,128]{0,1:T(8,128)(4,1)S(1)}, pred[128,128]{0,1:T(8,128)(4,1)}, u32[]{:S(2)}) copy-start(pred[128,128]{0,1:T(8,128)(4,1)} %copy-done.6) | copy-start | bytes 49156
  318.3 27.7 %copy-start.11 = (s32[128]{0:T(128)S(1)}, s32[128]{0:T(128)}, u32[]{:S(2)}) copy-start(s32[128]{0:T(128)} %copy-done.10) | copy-start | bytes 1540
  344.3 28.5 %slice-start = ((bf16[2048,512]{0,1:T(8,128)(2,1)}), bf16[1024,512]{0,1:T(8,128)(2,1)S(1)}, s32[]{:S(2)}) async-start(bf16[2048,512]{0,1:T(8,128)(2,1)} %all-gather.8.cloned.1.call-done), calls=%async_computation.6 | async-start | bytes 2097152 | tf_op jit(solution)/shard_map/slice | solution.py:112
  344.3 176.3 %all-gather.12.cloned.1.call-start = ((), (), s32[]{:S(2)}) async-start(), calls=%async_computation.5 | async-start | bytes 4456448 | tf_op jit(solution)/shard_map/all_gather | solution.py:127
  373.7 31.7 %copy-start.3 = (f32[8,128,128]{2,1,0:T(8,128)S(1)}, f32[8,128,128]{2,1,0:T(8,128)}, u32[]{:S(2)}) copy-start(f32[8,128,128]{2,1,0:T(8,128)} %get-tuple-element.321) | copy-start | bytes 1572868
  379.2 1.4 copy-start.2
  408.1 19.9 %collective-permute-start = (bf16[128,1024]{0,1:T(8,128)(2,1)S(1)}, bf16[128,1024]{0,1:T(8,128)(2,1)S(1)}, u32[]{:S(2)}, u32[]{:S(2)}) collective-permute-start(bf16[128,1024]{0,1:T(8,128)(2,1)S(1)} %constant_dynamic-slice_fusion), channel_id=1, source_target_pairs={{0,0},{1,8},{2,16},{3,24},{4,32},{5,40},{6,48},{7,56},{8,1},{9,9},... | collective-permute-start | bytes 786440 | tf_op jit(solution)/shard_map/ppermute | solution.py:126
  428.0 0.7 copy-start.8
  574.8 3.7 copy-start.9
  574.8 3.7 copy-start.12
  578.5 26.4 %copy-start.1 = (bf16[64,128,128]{2,1,0:T(8,128)(2,1)S(1)}, bf16[64,128,128]{2,1,0:T(8,128)(2,1)}, u32[]{:S(2)}) copy-start(bf16[64,128,128]{2,1,0:T(8,128)(2,1)} %param.53) | copy-start | bytes 6291460
Sparse Core Ops, SparseCore 0:
  181.9 45.7 all-gather.5
  256.8 45.8 all-gather.7
  344.4 24.9 all-gather.9
  428.9 53.5 all-gather.11
where the time goes:
time: 620 us; the launch traced here: 612 us
  other arithmetic  227 us (37%)
  local copies, waits for them, and re-layouts  154 us (25%)
  waiting for transfers between devices  92.2 us (15%)
  matrix products  82.1 us (13%)
  starting transfers between devices  24 us (4%)
  blocking collectives  18.7 us (3%)
  between operations  14.5 us (2%)
    another operation x24, other arithmetic, shards(): factor = jnp.linalg.cholesky(symmetric)  100 us
    another operation x11, other arithmetic, shards(): lax.linalg.triangular_solve(factor, eye, left_side=True, lower=True)  80 us
    all_to_all x1, waiting for transfers between devices, shards(): lax.all_to_all(send_tiles.reshape(owners, CAP, width, width), ('frow', 'f...  76.1 us
    unnamed x32, local copies, waits for them, and re-layouts  64.4 us
    broadcast_in_dim x1, local copies, waits for them, and re-layouts, shards(): return result[None, :, None, :]  20.5 us
    all_gather x1, blocking collectives, shards(): lax.all_gather(first_column[:width].astype(jnp.bfloat16), 'fcol', axis=1,...  18.7 us
    dot_general x1, matrix products, subtract_product(): jnp.dot(row_factor, col_factor.T, precision=lax.Precision.HIGH, preferred...  17.7 us
    dot_general x1, matrix products, shards(): jnp.dot(rows_all, factor_inverse.T, precision=hi, preferred_element_type=...  16.6 us
  transfers between devices with their start and end apart: 7, of which 2 were waited for; matrix products, arithmetic and copies ran while one was open for 59% of the time, Pallas kernels for 0%

commit v1 on v0

--- a/solution.py
+++ b/solution.py
@@ -1,11 +1,22 @@
+import functools
 import jax
 import jax.numpy as jnp
 from jax import lax
 from jax.sharding import PartitionSpec as P
+from jax.lax import all_to_all, axis_size
 
 PW = 512
 NPANEL = 2
 CAP = 2
+
+
+def waves_read(message, axis_id):
+    extent = axis_size(axis_id)
+    copies = [extent if c == 1 else 1 for c in range(message.ndim)]
+    return all_to_all(jnp.tile(message, copies), axis_id, split_axis=1, concat_axis=1, tiled=True)
+
+
+balance_tails = functools.partial(waves_read, axis_id="fcol")
 
 
 def as_sent(x):
@@ -103,9 +114,7 @@
     global_cols = (local_cols // width * col_devs + col_here) * width + local_cols % width
     total = NPANEL * PW
     hi = lax.Precision.HIGH
-    first_row = lax.all_gather(
-        first_column[:width].astype(jnp.bfloat16), "fcol", axis=1, tiled=True
-    )[:, :total]
+    first_row = balance_tails(first_column[:width].astype(jnp.bfloat16))[:, :total]
     split = total // 2
     left = lax.all_gather(first_row[:, :split], "frow", axis=0, tiled=True)[:total]
     left, right_src, matrix = lax.optimization_barrier((left, first_row[:, split:], matrix))

time: 620 us -> 557 us (0.90)
  local copies, waits for them, and re-layouts: 154 us -> 95.4 us
    unnamed x32 -> x22, local copies, waits for them, and re-layouts: 64.4 us -> 41.5 us
    all_gather x1 -> x0, blocking collectives: 18.7 us -> none  [shards(): lax.all_gather(first_column[:width].astype(jnp.bfloat16), 'fcol', axis=1,...]
    all_to_all x0 -> x1, blocking collectives: none -> 14.8 us  [waves_read(): all_to_all(jnp.tile(message, copies), axis_id, split_axis=1, concat_axis=...]
    ppermute x1, waiting for transfers between devices: 16 us -> 3.89 us  [shards(): piece = lax.ppermute(piece, ('frow', 'fcol'), pairs)]
    all_to_all x1, waiting for transfers between devices: 76.1 us -> 85.8 us  [shards(): lax.all_to_all(send_tiles.reshape(owners, CAP, width, width), ('frow', 'f...]
    reshape x1 -> x0, local copies, waits for them, and re-layouts: 9.27 us -> none  [shards(): added = summed.reshape(row_blocks, col_blocks, width, width).transpose(0,...]
    broadcast_in_dim x1, local copies, waits for them, and re-layouts: 20.5 us -> 12.5 us  [shards(): return result[None, :, None, :]]
    another operation x11 -> x9, other arithmetic: 80 us -> 79.3 us  [shards(): lax.linalg.triangular_solve(factor, eye, left_side=True, lower=True)]
  transfers between devices with their start and end apart: 7 -> 7, of which waited for: 2 -> 2; matrix products, arithmetic and copies ran while one was open for 59% -> 60% of each run, Pallas kernels for 0% -> 0%
where the time goes in v1:
time: 557 us; the launch traced here: 549 us
  other arithmetic  223 us (40%)
  local copies, waits for them, and re-layouts  95.4 us (17%)
  waiting for transfers between devices  89.8 us (16%)
  matrix products  85.8 us (15%)
  starting transfers between devices  26.3 us (5%)
  blocking collectives  14.8 us (3%)
  between operations  14.3 us (3%)
    another operation x24, other arithmetic, shards(): factor = jnp.linalg.cholesky(symmetric)  99.9 us
    all_to_all x1, waiting for transfers between devices, shards(): lax.all_to_all(send_tiles.reshape(owners, CAP, width, width), ('frow', 'f...  85.8 us
    another operation x9, other arithmetic, shards(): lax.linalg.triangular_solve(factor, eye, left_side=True, lower=True)  79.3 us
    unnamed x22, local copies, waits for them, and re-layouts  41.5 us
    dot_general x1, matrix products, subtract_product(): jnp.dot(row_factor, col_factor.T, precision=lax.Precision.HIGH, preferred...  18 us
    add x1, other arithmetic, shards(): matrix = local + added  17.4 us
    all_to_all x1, blocking collectives, waves_read(): all_to_all(jnp.tile(message, copies), axis_id, split_axis=1, concat_axis=...  14.8 us
    dot_general x1, matrix products, shards(): jnp.dot(rows_all, factor_inverse.T, precision=hi, preferred_element_type=...  14.6 us
  transfers between devices with their start and end apart: 7, of which 2 were waited for; matrix products, arithmetic and copies ran while one was open for 60% of the time, Pallas kernels for 0%

profile of v1, /device:TPU:23, one launch (start us, length us, event | category | flops | bytes accessed | tf_op | source)
XLA Modules:
  0.0 549.3 jit_solution(12780367596143964777)
XLA Ops:
  11.4 10.6 %all-to-all-start = ((s32[128,1,2]{2,1,0:T(1,128)}), s32[128,1,2]{2,1,0:T(1,128)S(1)}, u32[]{:S(2)}, u32[]{:S(2)}) async-start(s32[128,1,2]{2,1,0:T(1,128)} %bitcast.4), calls=%async_computation | async-start | bytes 131072 | tf_op jit(solution)/shard_map/all_to_all | solution.py:88
  26.8 10.2 %gather_fusion.1 = bf16[256,128,128]{2,1,0:T(8,128)(2,1)} fusion(bf16[64,128,128]{2,1,0:T(8,128)(2,1)} %fusion.28, s32[1024]{0:T(1024)S(1)} %pad_clamp_fusion), kind=kCustom, calls=%fused_computation.1 | custom fusion | bytes 16778240 | tf_op jit(solution)/shard_map/jit(_take)/gather | solution.py:77
  37.0 7.4 %select_select_fusion = bf16[128,2,128,128]{3,2,1,0:T(8,128)(2,1)} fusion(bf16[128,2,128,128]{3,2,1,0:T(8,128)(2,1)} %bitcast.215, pred[128,2]{1,0:T(8,128)(4,1)S(1)} %compare_and_fusion, pred[128,2]{1,0:T(8,128)(4,1)S(1)} %broadcast_in_dim.106), kind=kLoop, calls=%fused_computation.8 | loop fusion | flops 8388608 | bytes 16777728 | tf_op jit(solution)/shard_map/jit(_where)/select_n | solution.py:75
  44.4 10.2 %all-to-all-start.1 = ((bf16[128,2,128,128]{3,2,1,0:T(8,128)(2,1)}), bf16[128,2,128,128]{3,2,1,0:T(8,128)(2,1)}, u32[]{:S(2)}, u32[]{:S(2)}) async-start(bf16[128,2,128,128]{3,2,1,0:T(8,128)(2,1)} %select_select_fusion), calls=%async_computation.1 | async-start | bytes 16777216 | tf_op jit(solution)/shard_map/all_to_all | solution.py:81
  55.2 10.7 %copy.218 = f32[1,1024,1,2048]{3,1,2,0:T(8,128)} copy(f32[1,1024,1,2048]{3,2,1,0:T(1,128)} %param.52) | data formatting | bytes 16777216
  67.3 85.8 %all-to-all-done.1 = bf16[128,2,128,128]{3,2,1,0:T(8,128)(2,1)} async-done(((bf16[128,2,128,128]{3,2,1,0:T(8,128)(2,1)}), bf16[128,2,128,128]{3,2,1,0:T(8,128)(2,1)}, u32[]{:S(2)}, u32[]{:S(2)}) %all-to-all-start.1) | async-done | bytes 8388640 | tf_op jit(solution)/shard_map/all_to_all | solution.py:81
  153.1 7.8 %fusion.139 = f32[8,16384]{1,0:T(8,128)S(1)} fusion(s32[256]{0:T(256)S(1)} %eq.128, s32[8]{0:T(128)S(1)} %iota_multiply_fusion, bf16[32,8,128,128]{3,2,1,0:T(8,128)(2,1)} %bitcast.78), kind=kOutput, calls=%fused_computation.235 | convolution fusion | flops 67110912 | bytes 8913952 | tf_op jit(solution)/shard_map/dot_general | solution.py:107
  162.3 14.8 %all_to_all.20 = bf16[128,8,128]{0,2,1:T(8,128)(2,1)S(1)} all-to-all(bf16[128,8,128]{0,2,1:T(8,128)(2,1)S(1)} %tile.2), channel_id=1, replica_groups=mesh['frow'=16,'fcol'=8] {'fcol'}, dimensions={1} | all-to-all | bytes 524288 | tf_op jit(solution)/shard_map/all_to_all | solution.py:16
  178.3 23.5 %copy.217 = bf16[32,8,128,128]{3,1,2,0:T(8,128)(2,1)} copy(bf16[32,8,128,128]{3,2,1,0:T(8,128)(2,1)} %bitcast.78) | data formatting | bytes 16777216
  201.8 11.9 %copy.142 = bf16[256,16384]{0,1:T(8,128)(2,1)} copy(bf16[256,16384]{1,0:T(8,128)(2,1)} %bitcast.216) | data formatting | bytes 16777216 | tf_op jit(solution)/shard_map/reshape | solution.py:108
  213.8 9.6 %fusion.90 = f32[8,16,128,128]{3,1,2,0:T(8,128)} fusion(bf16[128,128,256,1]{2,1,0,3:T(8,128)(2,1)} %bitcast.219, s32[8,16]{1,0:T(8,128)S(1)} %multiply_add_fusion, s32[256]{0:T(256)S(1)} %eq.128), kind=kOutput, calls=%fused_computation.114 | convolution fusion | flops 1073774592 | bytes 16778752 | tf_op jit(solution)/shard_map/dot_general | solution.py:96
  223.4 17.4 %bitcast_add_fusion = f32[1024,2048]{1,0:T(8,128)} fusion(f32[128,8,16,128]{3,2,1,0:T(8,128)} %bitcast.218, f32[1,1024,1,2048]{3,2,1,0:T(1,128)} %param.52), kind=kLoop, calls=%fused_computation.2 | loop fusion | flops 2097152 | bytes 25165824 | tf_op jit(solution)/shard_map/add | solution.py:104
  243.7 11.7 %cholesky.134 = f32[128,128]{1,0:T(8,128)S(1)} custom-call(f32[128,128]{1,0:T(8,128)S(1)} %copy.149), custom_call_target="Cholesky" | custom-call | tf_op jit(solution)/shard_map/jit(cholesky)/cholesky | solution.py:164
  256.8 9.8 %custom-call.12 = f32[1,128,128]{1,2,0:T(8,128)S(1)} custom-call(f32[1,128,128]{2,1,0:T(8,128)S(1)} %get-tuple-element.281), custom_call_target="InvertDiagBlocksLowerTriangular" | custom-call | tf_op jit(solution)/shard_map/triangular_solve/custom-call.0 | solution.py:165
  272.8 12.1 %cholesky.145 = f32[128,128]{1,0:T(8,128)S(1)} custom-call(f32[128,128]{1,0:T(8,128)S(1)} %copy.156), custom_call_target="Cholesky" | custom-call | tf_op jit(solution)/shard_map/jit(cholesky)/cholesky | solution.py:164
  286.8 9.8 %custom-call.13 = f32[1,128,128]{1,2,0:T(8,128)S(1)} custom-call(f32[1,128,128]{2,1,0:T(8,128)S(1)} %get-tuple-element.310), custom_call_target="InvertDiagBlocksLowerTriangular" | custom-call | tf_op jit(solution)/shard_map/triangular_solve/custom-call.0 | solution.py:165
  300.3 11.7 %cholesky.156 = f32[128,128]{1,0:T(8,128)S(1)} custom-call(f32[128,128]{1,0:T(8,128)S(1)} %copy.163), custom_call_target="Cholesky" | custom-call | tf_op jit(solution)/shard_map/jit(cholesky)/cholesky | solution.py:164
  314.0 9.8 %custom-call.14 = f32[1,128,128]{1,2,0:T(8,128)S(1)} custom-call(f32[1,128,128]{2,1,0:T(8,128)S(1)} %get-tuple-element.308), custom_call_target="InvertDiagBlocksLowerTriangular" | custom-call | tf_op jit(solution)/shard_map/triangular_solve/custom-call.0 | solution.py:165
  326.9 11.7 %cholesky.167 = f32[128,128]{1,0:T(8,128)S(1)} custom-call(f32[128,128]{1,0:T(8,128)S(1)} %fusion.105), custom_call_target="Cholesky" | custom-call | tf_op jit(solution)/shard_map/jit(cholesky)/cholesky | solution.py:164
  340.6 10.0 %custom-call.15 = f32[1,128,128]{1,2,0:T(8,128)S(1)} custom-call(f32[1,128,128]{2,1,0:T(8,128)S(1)} %get-tuple-element.306), custom_call_target="InvertDiagBlocksLowerTriangular" | custom-call | tf_op jit(solution)/shard_map/triangular_solve/custom-call.0 | solution.py:165
  353.3 5.5 fusion.31
  361.3 11.7 %cholesky.178 = f32[128,128]{1,0:T(8,128)S(1)} custom-call(f32[128,128]{1,0:T(8,128)S(1)} %fusion.103), custom_call_target="Cholesky" | custom-call | tf_op jit(solution)/shard_map/jit(cholesky)/cholesky | solution.py:164
  380.6 9.8 %custom-call.16 = f32[1,128,128]{1,2,0:T(8,128)S(1)} custom-call(f32[1,128,128]{2,1,0:T(8,128)S(1)} %get-tuple-element.304), custom_call_target="InvertDiagBlocksLowerTriangular" | custom-call | tf_op jit(solution)/shard_map/triangular_solve/custom-call.0 | solution.py:165
  399.3 11.7 %cholesky.189 = f32[128,128]{1,0:T(8,128)S(1)} custom-call(f32[128,128]{1,0:T(8,128)S(1)} %fusion.101), custom_call_target="Cholesky" | custom-call | tf_op jit(solution)/shard_map/jit(cholesky)/cholesky | solution.py:164
  412.9 9.8 %custom-call.17 = f32[1,128,128]{1,2,0:T(8,128)S(1)} custom-call(f32[1,128,128]{2,1,0:T(8,128)S(1)} %get-tuple-element.302), custom_call_target="InvertDiagBlocksLowerTriangular" | custom-call | tf_op jit(solution)/shard_map/triangular_solve/custom-call.0 | solution.py:165
  424.7 12.1 %cholesky.200 = f32[128,128]{1,0:T(8,128)S(1)} custom-call(f32[128,128]{1,0:T(8,128)S(1)} %fusion.99), custom_call_target="Cholesky" | custom-call | tf_op jit(solution)/shard_map/jit(cholesky)/cholesky | solution.py:164
  438.6 9.8 %custom-call.18 = f32[1,128,128]{1,2,0:T(8,128)S(1)} custom-call(f32[1,128,128]{2,1,0:T(8,128)S(1)} %get-tuple-element.300), custom_call_target="InvertDiagBlocksLowerTriangular" | custom-call | tf_op jit(solution)/shard_map/triangular_solve/custom-call.0 | solution.py:165
  450.2 11.7 %cholesky.211 = f32[128,128]{1,0:T(8,128)S(1)} custom-call(f32[128,128]{1,0:T(8,128)S(1)} %fusion.97), custom_call_target="Cholesky" | custom-call | tf_op jit(solution)/shard_map/jit(cholesky)/cholesky | solution.py:164
  463.8 9.8 %custom-call.19 = f32[1,128,128]{1,2,0:T(8,128)S(1)} custom-call(f32[1,128,128]{2,1,0:T(8,128)S(1)} %get-tuple-element.298), custom_call_target="InvertDiagBlocksLowerTriangular" | custom-call | tf_op jit(solution)/shard_map/triangular_solve/custom-call.0 | solution.py:165
  489.6 14.6 %fusion.2 = f32[3072,1024]{1,0:T(8,128)S(1)} fusion(bf16[2048,1024]{1,0:T(8,128)(2,1)S(1)} %bitcast.221, bf16[1024,1024]{1,0:T(8,128)(2,1)S(1)} %copy-done.9, f32[1,512,512]{2,1,0:T(8,128)S(1)} %copy-done.7, f32[1,512,512]{2,1,0:T(8,128)S(1)} %copy-done.6, f32[1,512,512]{2,1,0:T(8,128)S(1)} %fusion.35), kind=kOutput, calls=%fused_computation.9 | convolution fusion | flops 19344130048 | bytes 22020096 | tf_op jit(solution)/shard_map/dot_general | solution.py:211
  509.2 18.0 %fusion.15 = f32[1024,2048]{1,0:T(8,128)S(1)} fusion(f32[1024,2048]{1,0:T(8,128)} %bitcast_add_fusion, f32[3072,1024]{1,0:T(8,128)} %copy-done.4), kind=kOutput, calls=%fused_computation.27 | convolution fusion | flops 12886999040 | bytes 29360128 | tf_op jit(solution)/shard_map/dot_general | solution.py:47
  530.0 12.5 %copy.186 = f32[1,1024,1,2048]{3,2,1,0:T(1,128)} copy(f32[1,1024,1,2048]{3,1,2,0:T(8,128)S(1)} %select_bitcast_fusion) | data formatting | bytes 16777216 | tf_op jit(solution)/shard_map/broadcast_in_dim | solution.py:224
  (184 shorter events, 91.4 us)
Async XLA Ops:
  6.5 16.6 %copy-start = (bf16[64,128,128]{2,1,0:T(8,128)(2,1)S(1)}, bf16[64,128,128]{2,1,0:T(8,128)(2,1)}, u32[]{:S(2)}) copy-start(bf16[64,128,128]{2,1,0:T(8,128)(2,1)} %param.53) | copy-start | bytes 6291460
  11.4 33.0 %all-to-all-start = ((s32[128,1,2]{2,1,0:T(1,128)}), s32[128,1,2]{2,1,0:T(1,128)S(1)}, u32[]{:S(2)}, u32[]{:S(2)}) async-start(s32[128,1,2]{2,1,0:T(1,128)} %bitcast.4), calls=%async_computation | async-start | bytes 131072 | tf_op jit(solution)/shard_map/all_to_all | solution.py:88
  44.4 108.7 %all-to-all-start.1 = ((bf16[128,2,128,128]{3,2,1,0:T(8,128)(2,1)}), bf16[128,2,128,128]{3,2,1,0:T(8,128)(2,1)}, u32[]{:S(2)}, u32[]{:S(2)}) async-start(bf16[128,2,128,128]{3,2,1,0:T(8,128)(2,1)} %select_select_fusion), calls=%async_computation.1 | async-start | bytes 16777216 | tf_op jit(solution)/shard_map/all_to_all | solution.py:81
  54.6 186.1 %all-gather.6.cloned.1.call-start = ((), (), s32[]{:S(2)}) async-start(), calls=%async_computation.3 | async-start | bytes 2228224 | tf_op jit(solution)/shard_map/all_gather | solution.py:119
  162.1 39.7 %copy-start.5 = (bf16[1024,128]{1,0:T(8,128)(2,1)}, bf16[1024,128]{1,0:T(8,128)(2,1)S(1)}, u32[]{:S(2)}) copy-start(bf16[1024,128]{1,0:T(8,128)(2,1)S(1)} %slice_add_fusion) | copy-start | bytes 786436
  177.8 122.3 %all-gather.8.cloned.1.call-start = ((), (), s32[]{:S(2)}) async-start(), calls=%async_computation.4 | async-start | bytes 2228224 | tf_op jit(solution)/shard_map/all_gather | solution.py:121
  242.1 131.6 %all-gather.10.cloned.1.call-start = ((), (), s32[]{:S(2)}) async-start(), calls=%async_computation.5 | async-start | bytes 2359296 | tf_op jit(solution)/shard_map/all_gather | solution.py:124
  300.1 52.6 %slice-start = ((bf16[2048,512]{0,1:T(8,128)(2,1)}), bf16[1024,512]{0,1:T(8,128)(2,1)S(1)}, s32[]{:S(2)}) async-start(bf16[2048,512]{0,1:T(8,128)(2,1)} %all-gather.8.cloned.1.call-done), calls=%async_computation.7 | async-start | bytes 2097152 | tf_op jit(solution)/shard_map/slice | solution.py:121
  300.2 185.9 %all-gather.12.cloned.1.call-start = ((), (), s32[]{:S(2)}) async-start(), calls=%async_computation.6 | async-start | bytes 4456448 | tf_op jit(solution)/shard_map/all_gather | solution.py:136
  353.3 37.1 %copy-start.3 = (f32[8,128,128]{2,1,0:T(8,128)S(1)}, f32[8,128,128]{2,1,0:T(8,128)}, u32[]{:S(2)}) copy-start(f32[8,128,128]{2,1,0:T(8,128)} %get-tuple-element.327) | copy-start | bytes 1572868
  358.8 1.3 copy-start.2
  374.7 19.9 %collective-permute-start = (bf16[128,1024]{1,0:T(8,128)(2,1)S(1)}, bf16[128,1024]{1,0:T(8,128)(2,1)S(1)}, u32[]{:S(2)}, u32[]{:S(2)}) collective-permute-start(bf16[128,1024]{1,0:T(8,128)(2,1)S(1)} %constant_dynamic-slice_fusion), channel_id=1, source_target_pairs={{0,0},{1,8},{2,16},{3,24},{4,32},{5,40},{6,48},{7,56},{8,1},{9,9},... | collective-permute-start | bytes 786440 | tf_op jit(solution)/shard_map/ppermute | solution.py:135
  394.6 0.7 copy-start.8
  486.1 2.8 copy-start.6
  486.1 2.9 copy-start.7
  486.1 3.5 copy-start.9
  504.2 4.6 copy-start.4
  530.0 12.5 %copy-start.1 = (bf16[64,128,128]{2,1,0:T(8,128)(2,1)S(1)}, bf16[64,128,128]{2,1,0:T(8,128)(2,1)}, u32[]{:S(2)}) copy-start(bf16[64,128,128]{2,1,0:T(8,128)(2,1)} %param.53) | copy-start | bytes 6291460
Sparse Core Ops, SparseCore 0:
  177.9 46.6 all-gather.5
  242.2 47.1 all-gather.7
  300.3 28.9 all-gather.9
  395.5 51.5 all-gather.11
